TPU v7x, 128 devices: a whole 4x4x4 slice. The times are simulated.
128 devices in a mesh: row: 8 (over z_lo, y), col: 16 (over x, z_hi, core).
Axes of the slice: x: 4, y: 4, z: 4 (z_hi: 2, z_lo: 2; z = z_hi * 2 + z_lo), core: 2. Of those that a mesh axis runs over, the one named last changes fastest.
Arguments:
- tokens: bfloat16 [2048, 2304], P('row', 'col'), may hold values from -6 to 6
- gate_weight: bfloat16 [8, 2304, 5760], P(None, 'col', 'row'), may hold values from -0.125 to 0.125
- up_weight: bfloat16 [8, 2304, 5760], P(None, 'col', 'row'), may hold values from -0.125 to 0.125
- down_weight: bfloat16 [8, 5760, 2304], P(None, 'row', 'col'), may hold values from -0.078125 to 0.078125
- route_ids: int32 [2048, 2], replicated, may hold values from 0 to 7, all different within a row; in each aligned block of 2048 rows (0 to 2047, 2048 to 4095, ...) at most 1024 rows name the same one
- route_weight: float32 [2048, 2], replicated, may hold values from 0.2 to 1
- prefill_cache: bfloat16 [2, 2048, 16, 2304], P(None, ('row', 'col')), may hold values from -6 to 6
- dest_col: int32 [8, 16, 16], P('row'), may hold values from 0 to 15, as said below
- dest_slot: int32 [8, 16, 16], P('row'), may hold values from 0 to 15, as said below
- pages_used: int32 [8, 16], P('row'), may hold values from 4 to 16, as said below
Outputs:
- mixed: bfloat16 [2048, 2304], P('row', 'col')
- decode_cache: bfloat16 [2, 2048, 16, 2304], P(None, ('row', 'col'))
Inputs may be any that keep to these rules, and one draw needn't show every extreme that they name: `route_ids`: each token names two different experts; no expert is named by more than 1024 tokens, a bound that some block reaches. For every device (r, c), dest_col[r, c, :] names each col index exactly 1 times. For every r and col index c2, the page slots of row r with dest_col = c2 carry distinct dest_slot values, so they fill all 16 slots of device (r, c2). The live slots of a device are its first pages_used slots; some device has all 16 live.
All inputs are finite; a program needn't handle non-finite values.
Results may differ from a plain program's by a relative error of at most 0.03.
Values may be sent and summed in bfloat16 or wider, within the bound.
No kernel may reach another device: no remote copies, remote signals or barrier semaphores. Data moves between devices by JAX's collectives and lax.ppermute only.
A program may use at most 192 MiB of HBM per device.

v0:
```python
import jax
import jax.numpy as jnp
from jax import lax
from jax.sharding import PartitionSpec as P


def aligned_apply(slot_rows, weights):
    experts = weights.shape[0]
    shaped = slot_rows.reshape(experts, -1, slot_rows.shape[1])
    product = jnp.einsum("ecd,edf->ecf", shaped, weights, preferred_element_type=jnp.float32)
    return product.reshape(-1, weights.shape[2])


def move_pages(prefill_cache, dest_col, dest_slot, pages_used):
    col_devices = lax.axis_size("col")
    own_index = lax.axis_index("col")
    slot_count = prefill_cache.shape[1]
    per_peer = slot_count // col_devices
    dest_table = dest_col[0]
    targets = dest_slot[0]
    page_index = jnp.arange(slot_count, dtype=jnp.int32)
    same_dest = dest_table[:, :, None] == dest_table[:, None, :]
    earlier = page_index[None, :] < page_index[:, None]
    dest_rank = jnp.sum((same_dest & earlier[None]).astype(jnp.int32), axis=2)
    send_order = lax.dynamic_index_in_dim(
        dest_table * per_peer + dest_rank, own_index, 0, keepdims=False
    )
    inverse = jnp.zeros((slot_count,), jnp.int32).at[send_order].set(page_index)
    own_used = lax.dynamic_index_in_dim(pages_used[0], own_index, 0, keepdims=False)
    is_live = page_index < own_used
    masked_pages = jnp.where(
        is_live[None, :, None, None], prefill_cache, jnp.zeros((), prefill_cache.dtype)
    )
    received = lax.all_to_all(
        masked_pages[:, inverse], "col", split_axis=1, concat_axis=1, tiled=True
    )
    senders = jnp.arange(col_devices, dtype=jnp.int32)[:, None]
    arrival = jnp.where(dest_table == own_index, senders * per_peer + dest_rank, slot_count)
    slot_of_arrival = (
        jnp.zeros((slot_count + 1,), jnp.int32)
        .at[arrival.reshape(-1)]
        .set(targets.reshape(-1))[:slot_count]
    )
    source_of_slot = jnp.zeros((slot_count,), jnp.int32).at[slot_of_arrival].set(page_index)
    return received[:, source_of_slot]


def shards(
    tokens,
    gate_weight,
    up_weight,
    down_weight,
    route_ids,
    route_weight,
    prefill_cache,
    dest_col,
    dest_slot,
    pages_used,
):
    decode_cache = move_pages(prefill_cache, dest_col, dest_slot, pages_used)
    gathered = lax.all_gather(tokens, "row", axis=0, tiled=True)
    token_count = route_ids.shape[0]
    assignments = token_count * 2
    capacity = token_count // 2
    experts = gate_weight.shape[0]
    flat_expert = route_ids.reshape(-1)
    labels = jnp.arange(experts, dtype=jnp.int32)
    assign_index = jnp.arange(assignments, dtype=jnp.int32)
    paired = jnp.concatenate([gate_weight, up_weight], axis=2)
    onehot = (flat_expert[:, None] == labels[None, :]).astype(jnp.int32)
    position = jnp.sum(jnp.cumsum(onehot, axis=0) * onehot, axis=1) - 1
    slot_of_assign = flat_expert * capacity + position
    row_assign = (
        jnp.full((experts * capacity,), assignments, jnp.int32).at[slot_of_assign].set(assign_index)
    )
    row_token = row_assign // 2
    padded_tokens = jnp.concatenate(
        [gathered, jnp.zeros((1, gathered.shape[1]), gathered.dtype)], axis=0
    )
    slot_rows = padded_tokens[row_token]
    weights_flat = jnp.concatenate([route_weight.reshape(-1), jnp.zeros((1,), jnp.float32)])
    row_weight = weights_flat[row_assign]
    partial_sums = aligned_apply(slot_rows, paired)
    summed = lax.psum_scatter(
        partial_sums.astype(jnp.bfloat16), "col", scatter_dimension=0, tiled=True
    ).astype(jnp.float32)
    share_rows = summed.shape[0]
    hidden_width = gate_weight.shape[2]
    own_weight = lax.dynamic_slice_in_dim(
        row_weight, lax.axis_index("col") * share_rows, share_rows, 0
    )
    hidden = (
        own_weight[:, None] * jax.nn.silu(summed[:, :hidden_width]) * summed[:, hidden_width:]
    ).astype(jnp.bfloat16)
    hidden_all = lax.all_gather(hidden, "col", axis=0, tiled=True)
    down_rows = aligned_apply(hidden_all, down_weight)
    pair_slots = slot_of_assign.reshape(token_count, 2)
    per_token = down_rows[pair_slots[:, 0]] + down_rows[pair_slots[:, 1]]
    mixed = lax.psum_scatter(per_token.astype(jnp.bfloat16), "row", scatter_dimension=0, tiled=True)
    return (mixed, decode_cache)


def solution(mesh):
    in_specs = (
        P("row", "col"),
        P(None, "col", "row"),
        P(None, "col", "row"),
        P(None, "row", "col"),
        P(),
        P(),
        P(None, ("row", "col"), None, None),
        P("row", None, None),
        P("row", None, None),
        P("row", None),
    )
    out_specs = (P("row", "col"), P(None, ("row", "col"), None, None))
    return jax.shard_map(shards, mesh=mesh, in_specs=in_specs, out_specs=out_specs, check_vma=False)
```

profile of v0, /device:TPU:0, one launch (start us, length us, event | category | flops | bytes accessed | tf_op | source)
XLA Modules:
  0.0 519.4 jit_solution(9502357657079924522)
XLA Ops:
  7.2 1.2 copy.43
  9.4 2.3 reduce-window.6
  12.4 2.0 sub.17
  14.4 2.8 fusion.28
  17.2 1.8 mul.40
  19.1 15.5 %scatter_custom_fusion = s32[8192]{0:T(1024)S(1)} fusion(s32[4096]{0:T(1024)S(1)} %bitcast.51, s32[4096]{0:T(1024)S(1)} %iota.35, s32[]{:T(128)} %constant.20.clone.1), kind=kCustom, calls=%fused_computation.48 | custom fusion | bytes 32772 | tf_op jit(solution)/shard_map/scatter | solution.py:74
  34.8 31.4 %all_gather.6 = bf16[2048,144]{1,0:T(8,128)(2,1)S(1)} all-gather(bf16[256,144]{1,0:T(8,128)(2,1)S(1)} %copy.46), channel_id=1, replica_groups=mesh['row'=8,'col'=16] {'row'}, dimensions={0}, use_global_device_ids=true | all-gather | bytes 663552 | tf_op jit(solution)/shard_map/all_gather | solution.py:61
  66.4 32.9 %gather_fusion.1 = bf16[8192,144]{1,0:T(8,128)(2,1)} fusion(bf16[2049,144]{1,0:T(8,128)(2,1)S(1)} %concatenate.10, s32[8192]{0:T(1024)S(1)} %get-tuple-element.15), kind=kCustom, calls=%fused_computation.1 | custom fusion | bytes 4751360 | tf_op jit(solution)/shard_map/gather | solution.py:80
  99.3 15.6 %convert_bitcast_fusion = bf16[8,180,8,1024]{3,2,1,0:T(8,128)(2,1)} fusion(bf16[8,1024,144]{2,1,0:T(8,128)(2,1)} %bitcast.44, bf16[8,144,720]{2,1,0:T(8,128)(2,1)} %param.12, bf16[8,144,720]{2,1,0:T(8,128)(2,1)} %param.11), kind=kOutput, calls=%fused_computation.10 | convolution fusion | flops 3415818240 | bytes 29270016 | tf_op jit(solution)/shard_map/ecd,edf->ecf/dot_general | solution.py:10
  114.9 20.1 %copy.60 = bf16[8,180,8,1024]{3,2,0,1:T(8,128)(2,1)} copy(bf16[8,180,8,1024]{3,2,1,0:T(8,128)(2,1)} %convert_bitcast_fusion) | data formatting | bytes 47185920 | tf_op jit(solution)/shard_map/convert_element_type | solution.py:85
  135.0 0.6 copy-done.4
  136.5 45.5 %gather_fusion = f32[8192]{0:T(1024)S(1)} fusion(f32[4097]{0:T(1024)S(1)} %pad_maximum_fusion, s32[8192]{0:T(1024)S(1)} %get-tuple-element.14), kind=kCustom, calls=%fused_computation | custom fusion | bytes 98304 | tf_op jit(solution)/shard_map/gather | solution.py:82
  182.2 135.9 %reduce-scatter.3.cloned.1.call-done = bf16[512,1440]{0,1:T(8,128)(2,1)} async-done(((bf16[8192,1440]{0,1:T(8,128)(2,1)}), bf16[512,1440]{0,1:T(8,128)(2,1)}) %reduce-scatter.3.cloned.1.call-update) | async-done | bytes 1474576 | tf_op jit(solution)/shard_map/reduce_scatter | solution.py:84
  318.0 1.8 convert_element_type.26
  319.9 1.4 fusion.6
  322.6 0.6 scatter_custom_fusion.1
  323.2 1.6 scatter_custom_fusion.2
  324.8 0.7 iota_compare_fusion.3
  325.5 3.3 broadcast_select_fusion
  328.8 3.9 gather_fusion.4
  332.7 4.6 all-to-all-start
  337.4 0.9 fusion.8
  338.3 96.2 %all-gather.2.cloned.1.call-done = bf16[8192,720]{0,1:T(8,128)(2,1)} async-done(((bf16[512,720]{0,1:T(8,128)(2,1)}), bf16[8192,720]{0,1:T(8,128)(2,1)}) %all-gather.2.cloned.1.call-update) | async-done | bytes 11796496 | tf_op jit(solution)/shard_map/all_gather | solution.py:95
  434.5 11.5 %fusion = f32[8,1024,144]{2,1,0:T(8,128)} fusion(bf16[8,720,144]{1,2,0:T(8,128)(2,1)S(1)} %copy-done, bf16[90,8,8,1024]{3,2,1,0:T(8,128)(2,1)} %bitcast.53), kind=kOutput, calls=%fused_computation.11 | convolution fusion | flops 1698693120 | bytes 18173952 | tf_op jit(solution)/shard_map/reshape | solution.py:11
  446.0 11.9 %gather_fusion.3 = f32[2048,144]{1,0:T(8,128)} fusion(f32[8192,144]{1,0:T(8,128)} %bitcast.41, s32[2048]{0:T(1024)S(1)} %get-tuple-element.18), kind=kCustom, calls=%fused_computation.3 | custom fusion | bytes 2367488 | tf_op jit(solution)/shard_map/gather | solution.py:98
  458.0 12.0 %gather_fusion.2 = f32[2048,144]{1,0:T(8,128)} fusion(f32[8192,144]{1,0:T(8,128)} %bitcast.42, s32[2048]{0:T(1024)S(1)} %get-tuple-element.19), kind=kCustom, calls=%fused_computation.2 | custom fusion | bytes 2367488 | tf_op jit(solution)/shard_map/gather | solution.py:98
  469.9 3.4 add_convert_fusion
  474.0 3.2 copy.53
  477.3 3.8 gather_fusion.5
  481.1 3.2 copy.55
  484.3 26.9 %reduce-scatter.5.cloned.1.call-done = bf16[256,144]{1,0:T(8,128)(2,1)} async-done(((bf16[2048,144]{1,0:T(8,128)(2,1)}), bf16[256,144]{1,0:T(8,128)(2,1)}) %reduce-scatter.5.cloned.1.call-update) | async-done | bytes 73744 | tf_op jit(solution)/shard_map/reduce_scatter | solution.py:99
  511.2 1.6 copy.54
  (55 shorter events, 5.1 us)
Async XLA Ops:
  7.2 427.3 %copy-start = (bf16[8,720,144]{1,2,0:T(8,128)(2,1)S(1)}, bf16[8,720,144]{1,2,0:T(8,128)(2,1)}, u32[]{:S(2)}) copy-start(bf16[8,720,144]{1,2,0:T(8,128)(2,1)} %param.13) | copy-start | bytes 4976644
  7.2 310.9 %reduce-scatter.3.cloned.1.call-start = ((), (), s32[]{:S(2)}) async-start(), calls=%async_computation.3 | async-start | bytes 25067520 | tf_op jit(solution)/shard_map/reduce_scatter | solution.py:84
  14.4 20.3 %copy-start.3 = (bf16[256,144]{0,1:T(8,128)(2,1)S(1)}, bf16[256,144]{0,1:T(8,128)(2,1)}, u32[]{:S(2)}) copy-start(bf16[256,144]{0,1:T(8,128)(2,1)} %param.10) | copy-start | bytes 221188
  135.0 0.7 copy-start.4
  135.0 299.5 %all-gather.2.cloned.1.call-start = ((), (), s32[]{:S(2)}) async-start(), calls=%async_computation.4 | async-start | bytes 12533760 | tf_op jit(solution)/shard_map/all_gather | solution.py:95
  319.8 1.4 copy-start.2
  319.8 2.1 copy-start.5
  319.8 2.1 copy-start.6
  332.7 4.6 copy-start.1
  332.7 141.3 %all-to-all-start = ((bf16[2,16,16,2304]{3,2,0,1:T(8,128)(2,1)}), bf16[2,16,16,2304]{3,2,0,1:T(8,128)(2,1)}, u32[]{:S(2)}, u32[]{:S(2)}) async-start(bf16[2,16,16,2304]{3,2,0,1:T(8,128)(2,1)} %bitcast.45), calls=%async_computation.2 | async-start | bytes 4718592 | tf_op jit(solution)/shard_map/all_to_all | solution.py:34
  337.3 173.9 %reduce-scatter.5.cloned.1.call-start = ((), (), s32[]{:S(2)}) async-start(), calls=%async_computation.5 | async-start | bytes 1179648 | tf_op jit(solution)/shard_map/reduce_scatter | solution.py:99
Sparse Core Ops, SparseCore 0:
  135.1 182.8 reduce-scatter.2
  321.4 113.0 all-gather.1
  473.5 37.7 reduce-scatter.4
where the time goes:
time: 520 us; the launch traced here: 519 us
  waiting for transfers between devices  259 us (50%)
  local copies, waits for them, and re-layouts  166 us (32%)
  blocking collectives  31.4 us (6%)
  matrix products  27.1 us (5%)
  other arithmetic  17.4 us (3%)
  between operations  14.1 us (3%)
    reduce_scatter x1, waiting for transfers between devices, shards(): lax.psum_scatter(partial_sums.astype(jnp.bfloat16), 'col', scatter_dimens...  136 us
    all_gather x1, waiting for transfers between devices, shards(): hidden_all = lax.all_gather(hidden, 'col', axis=0, tiled=True)  96.2 us
    gather x1, local copies, waits for them, and re-layouts, shards(): row_weight = weights_flat[row_assign]  45.5 us
    gather x1, local copies, waits for them, and re-layouts, shards(): slot_rows = padded_tokens[row_token]  32.9 us
    all_gather x1, blocking collectives, shards(): gathered = lax.all_gather(tokens, 'row', axis=0, tiled=True)  31.4 us
    reduce_scatter x1, waiting for transfers between devices, shards(): lax.psum_scatter(per_token.astype(jnp.bfloat16), 'row', scatter_dimension...  26.9 us
    gather x2, local copies, waits for them, and re-layouts, shards(): per_token = down_rows[pair_slots[:, 0]] + down_rows[pair_slots[:, 1]]  23.9 us
    convert_element_type x1, local copies, waits for them, and re-layouts, shards(): partial_sums.astype(jnp.bfloat16)  20.1 us
  transfers between devices with their start and end apart: 4, of which 3 were waited for; matrix products, arithmetic and copies ran while one was open for 21% of the time, Pallas kernels for 0%

commit v1 on v0

--- a/solution.py
+++ b/solution.py
@@ -1,7 +1,17 @@
+import functools
 import jax
 import jax.numpy as jnp
 from jax import lax
 from jax.sharding import PartitionSpec as P
+
+
+def trace_wall_by_axis(tile_in, dev_axis):
+    a_now = jnp.stack([tile_in for _ in range(lax.axis_size(dev_axis))], 0)
+    val2 = lax.all_to_all(a_now, dev_axis, 0, 0)
+    return jnp.concatenate(val2, 0)
+
+
+put_circles_in = functools.partial(trace_wall_by_axis, dev_axis="col")
 
 
 def aligned_apply(slot_rows, weights):
@@ -92,7 +102,7 @@
     hidden = (
         own_weight[:, None] * jax.nn.silu(summed[:, :hidden_width]) * summed[:, hidden_width:]
     ).astype(jnp.bfloat16)
-    hidden_all = lax.all_gather(hidden, "col", axis=0, tiled=True)
+    hidden_all = put_circles_in(hidden)
     down_rows = aligned_apply(hidden_all, down_weight)
     pair_slots = slot_of_assign.reshape(token_count, 2)
     per_token = down_rows[pair_slots[:, 0]] + down_rows[pair_slots[:, 1]]

time: 520 us -> 663 us (1.27)
  waiting for transfers between devices: 259 us -> 341 us
  local copies, waits for them, and re-layouts: 166 us -> 209 us
  matrix products: 27.1 us -> 37.3 us
  starting transfers between devices: 4.7 us -> 12.7 us
    all_to_all x0 -> x1, waiting for transfers between devices: none -> 175 us  [trace_wall_by_axis(): val2 = lax.all_to_all(a_now, dev_axis, 0, 0)]
    all_gather x1 -> x0, waiting for transfers between devices: 96.2 us -> none  [shards(): hidden_all = lax.all_gather(hidden, 'col', axis=0, tiled=True)]
    another operation x0 -> x2, local copies, waits for them, and re-layouts: none -> 23.4 us  [the longest x1 18 us: aligned_apply(): shaped = slot_rows.reshape(experts, -1, slot_rows.shape[1])]
    all_to_all x0 -> x1, local copies, waits for them, and re-layouts: none -> 19.8 us  [trace_wall_by_axis(): val2 = lax.all_to_all(a_now, dev_axis, 0, 0)]
    reshape x1, matrix products: 11.5 us -> 21.7 us  [aligned_apply(): return product.reshape(-1, weights.shape[2])]
  transfers between devices with their start and end apart: 4 -> 4, of which waited for: 3 -> 3; matrix products, arithmetic and copies ran while one was open for 21% -> 24% of each run, Pallas kernels for 0% -> 0%
where the time goes in v1:
time: 663 us; the launch traced here: 662 us
  waiting for transfers between devices  341 us (51%)
  local copies, waits for them, and re-layouts  209 us (32%)
  matrix products  37.3 us (6%)
  blocking collectives  31.4 us (5%)
  other arithmetic  16.6 us (3%)
  between operations  14.3 us (2%)
  starting transfers between devices  12.7 us (2%)
    all_to_all x1, waiting for transfers between devices, trace_wall_by_axis(): val2 = lax.all_to_all(a_now, dev_axis, 0, 0)  175 us
    reduce_scatter x1, waiting for transfers between devices, shards(): lax.psum_scatter(partial_sums.astype(jnp.bfloat16), 'col', scatter_dimens...  136 us
    gather x1, local copies, waits for them, and re-layouts, shards(): row_weight = weights_flat[row_assign]  45.5 us
    gather x1, local copies, waits for them, and re-layouts, shards(): slot_rows = padded_tokens[row_token]  32.9 us
    all_gather x1, blocking collectives, shards(): gathered = lax.all_gather(tokens, 'row', axis=0, tiled=True)  31.4 us
    reduce_scatter x1, waiting for transfers between devices, shards(): lax.psum_scatter(per_token.astype(jnp.bfloat16), 'row', scatter_dimension...  30.3 us
    gather x2, local copies, waits for them, and re-layouts, shards(): per_token = down_rows[pair_slots[:, 0]] + down_rows[pair_slots[:, 1]]  23.9 us
    reshape x1, matrix products, aligned_apply(): return product.reshape(-1, weights.shape[2])  21.7 us
  transfers between devices with their start and end apart: 4, of which 3 were waited for; matrix products, arithmetic and copies ran while one was open for 24% of the time, Pallas kernels for 0%

profile of v1, /device:TPU:0, one launch (start us, length us, event | category | flops | bytes accessed | tf_op | source)
XLA Modules:
  0.0 662.1 jit_solution(16806648994632972437)
XLA Ops:
  7.2 1.2 copy.58
  9.4 2.3 reduce-window.6
  12.4 2.0 sub.17
  14.4 2.8 fusion.27
  17.2 1.8 mul.40
  19.1 15.5 %scatter_custom_fusion = s32[8192]{0:T(1024)S(1)} fusion(s32[4096]{0:T(1024)S(1)} %bitcast.49, s32[4096]{0:T(1024)S(1)} %iota.35, s32[]{:T(128)} %constant.20.clone.1), kind=kCustom, calls=%fused_computation.47 | custom fusion | bytes 32772 | tf_op jit(solution)/shard_map/scatter | solution.py:84
  34.8 31.4 %all_gather.3 = bf16[2048,144]{1,0:T(8,128)(2,1)S(1)} all-gather(bf16[256,144]{1,0:T(8,128)(2,1)S(1)} %copy.61), channel_id=1, replica_groups=mesh['row'=8,'col'=16] {'row'}, dimensions={0}, use_global_device_ids=true | all-gather | bytes 663552 | tf_op jit(solution)/shard_map/all_gather | solution.py:71
  66.4 32.9 %gather_fusion.1 = bf16[8192,144]{1,0:T(8,128)(2,1)} fusion(bf16[2049,144]{1,0:T(8,128)(2,1)S(1)} %concatenate.10, s32[8192]{0:T(1024)S(1)} %get-tuple-element.17), kind=kCustom, calls=%fused_computation.1 | custom fusion | bytes 4751360 | tf_op jit(solution)/shard_map/gather | solution.py:90
  99.3 15.6 %convert_bitcast_fusion = bf16[8,180,8,1024]{3,2,1,0:T(8,128)(2,1)} fusion(bf16[8,1024,144]{2,1,0:T(8,128)(2,1)} %bitcast.42, bf16[8,144,720]{2,1,0:T(8,128)(2,1)} %param.12, bf16[8,144,720]{2,1,0:T(8,128)(2,1)} %param.11), kind=kOutput, calls=%fused_computation.10 | convolution fusion | flops 3415818240 | bytes 29270016 | tf_op jit(solution)/shard_map/ecd,edf->ecf/dot_general | solution.py:20
  114.9 20.1 %copy.75 = bf16[8,180,8,1024]{3,2,0,1:T(8,128)(2,1)} copy(bf16[8,180,8,1024]{3,2,1,0:T(8,128)(2,1)} %convert_bitcast_fusion) | data formatting | bytes 47185920 | tf_op jit(solution)/shard_map/convert_element_type | solution.py:95
  136.5 45.5 %gather_fusion = f32[8192]{0:T(1024)S(1)} fusion(f32[4097]{0:T(1024)S(1)} %pad_maximum_fusion, s32[8192]{0:T(1024)S(1)} %get-tuple-element.16), kind=kCustom, calls=%fused_computation | custom fusion | bytes 98304 | tf_op jit(solution)/shard_map/gather | solution.py:92
  182.2 135.9 %reduce-scatter.3.cloned.1.call-done = bf16[512,1440]{0,1:T(8,128)(2,1)} async-done(((bf16[8192,1440]{0,1:T(8,128)(2,1)}), bf16[512,1440]{0,1:T(8,128)(2,1)}) %reduce-scatter.3.cloned.1.call-update) | async-done | bytes 1474576 | tf_op jit(solution)/shard_map/reduce_scatter | solution.py:94
  318.0 1.8 convert_element_type.26
  320.3 5.4 stack.2
  325.7 5.0 all-to-all-start
  332.9 1.4 scatter_custom_fusion.2
  335.0 3.3 broadcast_select_fusion
  338.3 3.9 gather_fusion.4
  342.3 0.9 fusion.7
  343.2 174.6 %all-to-all-done = bf16[16,512,720]{1,2,0:T(8,128)(2,1)} async-done(((bf16[16,512,720]{1,2,0:T(8,128)(2,1)}), bf16[16,512,720]{1,2,0:T(8,128)(2,1)}, u32[]{:S(2)}, u32[]{:S(2)}) %all-to-all-start) | async-done | bytes 11796512 | tf_op jit(solution)/shard_map/all_to_all | solution.py:10
  517.8 7.6 %all-to-all-start.1 = ((bf16[2,16,16,2304]{3,2,0,1:T(8,128)(2,1)}), bf16[2,16,16,2304]{3,2,0,1:T(8,128)(2,1)}, u32[]{:S(2)}, u32[]{:S(2)}) async-start(bf16[2,16,16,2304]{3,2,0,1:T(8,128)(2,1)} %bitcast.43), calls=%async_computation.3 | async-start | bytes 4718592 | tf_op jit(solution)/shard_map/all_to_all | solution.py:44
  525.4 19.8 %copy.64 = bf16[16,512,720]{1,0,2:T(8,128)(2,1)} copy(bf16[16,512,720]{1,2,0:T(8,128)(2,1)} %all-to-all-done) | data formatting | bytes 23592960 | tf_op jit(solution)/shard_map/all_to_all | solution.py:10
  545.3 18.0 %reshape_reshape.3 = bf16[8,1024,720]{1,0,2:T(8,128)(2,1)} reshape(bf16[16,512,720]{1,0,2:T(8,128)(2,1)} %copy.64) | data formatting | bytes 23592960 | tf_op jit(solution)/shard_map/reshape;reshape | solution.py:19
  563.3 21.7 %fusion = f32[8,1024,144]{2,1,0:T(8,128)} fusion(bf16[8,720,144]{1,2,0:T(8,128)(2,1)S(1)} %copy-done, bf16[8,1024,720]{1,0,2:T(8,128)(2,1)} %reshape_reshape.3), kind=kOutput, calls=%fused_computation.11 | convolution fusion | flops 1698693120 | bytes 18173952 | tf_op jit(solution)/shard_map/reshape | solution.py:21
  585.0 11.9 %gather_fusion.3 = f32[2048,144]{1,0:T(8,128)} fusion(f32[8192,144]{1,0:T(8,128)} %bitcast.39, s32[2048]{0:T(1024)S(1)} %get-tuple-element.20), kind=kCustom, calls=%fused_computation.3 | custom fusion | bytes 2367488 | tf_op jit(solution)/shard_map/gather | solution.py:108
  596.9 12.0 %gather_fusion.2 = f32[2048,144]{1,0:T(8,128)} fusion(f32[8192,144]{1,0:T(8,128)} %bitcast.40, s32[2048]{0:T(1024)S(1)} %get-tuple-element.21), kind=kCustom, calls=%fused_computation.2 | custom fusion | bytes 2367488 | tf_op jit(solution)/shard_map/gather | solution.py:108
  608.9 3.4 add_convert_fusion
  613.0 3.2 copy.69
  616.3 3.8 gather_fusion.5
  620.0 3.2 copy.71
  623.3 30.3 %reduce-scatter.5.cloned.1.call-done = bf16[256,144]{1,0:T(8,128)(2,1)} async-done(((bf16[2048,144]{1,0:T(8,128)(2,1)}), bf16[256,144]{1,0:T(8,128)(2,1)}) %reduce-scatter.5.cloned.1.call-update) | async-done | bytes 73744 | tf_op jit(solution)/shard_map/reduce_scatter | solution.py:109
  653.6 1.6 copy.70
  (57 shorter events, 7.7 us)
Async XLA Ops:
  7.2 556.1 %copy-start = (bf16[8,720,144]{1,2,0:T(8,128)(2,1)S(1)}, bf16[8,720,144]{1,2,0:T(8,128)(2,1)}, u32[]{:S(2)}) copy-start(bf16[8,720,144]{1,2,0:T(8,128)(2,1)} %param.13) | copy-start | bytes 4976644
  7.2 310.9 %reduce-scatter.3.cloned.1.call-start = ((), (), s32[]{:S(2)}) async-start(), calls=%async_computation.4 | async-start | bytes 25067520 | tf_op jit(solution)/shard_map/reduce_scatter | solution.py:94
  14.4 20.3 %copy-start.3 = (bf16[256,144]{0,1:T(8,128)(2,1)S(1)}, bf16[256,144]{0,1:T(8,128)(2,1)}, u32[]{:S(2)}) copy-start(bf16[256,144]{0,1:T(8,128)(2,1)} %param.10) | copy-start | bytes 221188
  135.0 0.7 copy-start.4
  325.7 5.0 copy-start.2
  325.7 5.7 copy-start.5
  325.7 5.8 copy-start.6
  325.7 192.0 %all-to-all-start = ((bf16[16,512,720]{1,2,0:T(8,128)(2,1)}), bf16[16,512,720]{1,2,0:T(8,128)(2,1)}, u32[]{:S(2)}, u32[]{:S(2)}) async-start(bf16[16,512,720]{1,2,0:T(8,128)(2,1)} %stack.2), calls=%async_computation.1 | async-start | bytes 23592960 | tf_op jit(solution)/shard_map/all_to_all | solution.py:10
  338.3 3.9 copy-start.1
  517.8 95.3 %all-to-all-start.1 = ((bf16[2,16,16,2304]{3,2,0,1:T(8,128)(2,1)}), bf16[2,16,16,2304]{3,2,0,1:T(8,128)(2,1)}, u32[]{:S(2)}, u32[]{:S(2)}) async-start(bf16[2,16,16,2304]{3,2,0,1:T(8,128)(2,1)} %bitcast.43), calls=%async_computation.3 | async-start | bytes 4718592 | tf_op jit(solution)/shard_map/all_to_all | solution.py:44
  525.4 128.2 %reduce-scatter.5.cloned.1.call-start = ((), (), s32[]{:S(2)}) async-start(), calls=%async_computation.5 | async-start | bytes 1179648 | tf_op jit(solution)/shard_map/reduce_scatter | solution.py:109
Sparse Core Ops, SparseCore 0:
  135.1 182.8 reduce-scatter.2
  612.5 41.0 reduce-scatter.4
